TPU v7x, 128 devices: a whole 4x4x4 slice. The times are simulated.
128 devices in a mesh: row: 8 (over x, y_hi), col: 16 (over y_lo, z, core).
Axes of the slice: x: 4, y: 4 (y_hi: 2, y_lo: 2; y = y_hi * 2 + y_lo), z: 4, core: 2. Of those that a mesh axis runs over, the one named last changes fastest.
Arguments:
- flat_gradient: bfloat16 [8, 16, 524288], P('row', 'col'), may hold values from -6 to 6
- range_rows: int32 [8, 16], replicated, may hold values from 1 to 64, 512 in all within a row
- left_stat: float32 [4096, 4096], P('row', 'col'), may hold values from -6 to 6
- right_stat: float32 [8192, 8192], P('col', 'row'), may hold values from -6 to 6
- left_root: bfloat16 [4096, 4096], P('row'), as said below
- right_root: bfloat16 [8192, 8192], P('col'), as said below
Outputs:
- left_new: float32 [4096, 4096], P('row', 'col')
- right_new: float32 [8192, 8192], P('col', 'row')
- update: bfloat16 [4096, 8192], P('row', 'col')
Inputs may be any that keep to these rules, and one draw needn't show every extreme that they name: In each row r the entries sum to 512; the largest entry of every row is exactly 64. Slots of flat_gradient beyond a device's range_rows rows are padding. left_root equals its transpose. right_root equals its transpose.
All inputs are finite; a program needn't handle non-finite values.
Results may differ from a plain program's by a relative error of at most 0.014.
Values may be sent and summed in bfloat16 or wider, within the bound.
No kernel may reach another device: no remote copies, remote signals or barrier semaphores. Data moves between devices by JAX's collectives and lax.ppermute only.
A program may use at most 192 MiB of HBM per device.

v0:
```python
import math
import jax
import jax.numpy as jnp
from jax import lax
from jax.sharding import Mesh
from jax.sharding import PartitionSpec as P

HQ = 4096
DIN = 8192
stat_decay = 0.9
COL = ("chip", "core")
ROW = ("x", "yh")


def slot_index(row_counts, tile_rows, capacity):
    offsets = jnp.cumsum(row_counts) - row_counts
    target = jnp.arange(tile_rows, dtype=jnp.int32)
    covered = target[:, None] >= offsets[None, :]
    source = jnp.sum(covered.astype(jnp.int32), axis=1) - 1
    begins = jnp.max(jnp.where(covered, offsets[None, :], 0), axis=1)
    return source * capacity + target - begins


def partner(block):
    return lax.ppermute(block, "core", [(0, 1), (1, 0)])


def shards(flat_gradient, range_rows, left_stat, right_stat, left_root, right_root):
    x_count = lax.axis_size("x")
    row_count = x_count * 2
    chip_count = lax.axis_size("chip")
    col_count = chip_count * 2
    row_index = lax.axis_index(ROW)
    x_index = lax.axis_index("x")
    y_half = lax.axis_index("yh")
    core = lax.axis_index("core")
    tile_rows = HQ // row_count
    tile_cols = DIN // col_count
    slice_rows = tile_rows // col_count
    block_cols = DIN // row_count
    chunk = HQ // col_count
    capacity = flat_gradient.shape[2] // DIN
    held_rows = flat_gradient.reshape(capacity, DIN)
    received = lax.all_to_all(held_rows, COL, split_axis=1, concat_axis=0, tiled=True)
    row_counts = lax.dynamic_index_in_dim(range_rows, row_index, 0, keepdims=False)
    grad_tile = jnp.take(received, slot_index(row_counts, tile_rows, capacity), axis=0)
    row_slice = lax.all_to_all(grad_tile, COL, split_axis=0, concat_axis=1, tiled=True)
    block_piece = lax.all_to_all(row_slice, ROW, split_axis=1, concat_axis=0, tiled=True)
    other_half = lax.ppermute(grad_tile, "yh", [(0, 1), (1, 0)])
    other_half, block_piece = lax.optimization_barrier((other_half, block_piece))
    first = jnp.where(y_half == 0, grad_tile, other_half)
    second = jnp.where(y_half == 0, other_half, grad_tile)
    pair = jnp.stack([first, second])
    moved = [
        lax.ppermute(pair, "x", [(i, (i + s) % x_count) for i in range(x_count)])
        for s in range(1, x_count)
    ]
    row_block = lax.all_gather(block_piece, COL, axis=0, tiled=True)
    panel_parts = jnp.zeros((row_count, tile_rows, tile_cols), grad_tile.dtype)
    panel_parts = lax.dynamic_update_slice_in_dim(panel_parts, pair, 2 * x_index, 0)
    for s in range(1, x_count):
        panel_parts = lax.dynamic_update_slice_in_dim(
            panel_parts, moved[s - 1], 2 * ((x_index - s) % x_count), 0
        )
    column_panel = panel_parts.reshape(HQ, tile_cols)
    left_mixed = jnp.dot(left_root, column_panel, preferred_element_type=jnp.float32).astype(
        jnp.bfloat16
    )
    column_panel, left_mixed, row_block = lax.optimization_barrier(
        (column_panel, left_mixed, row_block)
    )
    col_index = lax.axis_index(COL)
    sub = jnp.arange(chunk, dtype=jnp.int32)
    sub_index = (
        (col_index % 2 * (col_count // 2) + sub // slice_rows) * (row_count * slice_rows)
        + col_index // 2 * slice_rows
        + sub % slice_rows
    )
    sub_rows = jnp.take(row_block, sub_index, axis=0)
    left_part = lax.dot_general(
        row_block, sub_rows, (((1,), (1,)), ((), ())), preferred_element_type=jnp.float32
    )
    left_part = left_part.reshape(col_count, row_count, slice_rows, chunk).transpose(1, 0, 2, 3)
    left_part = left_part.reshape(row_count, tile_rows, chunk)
    pair_parts = left_part.reshape(x_count, 2, tile_rows, chunk)
    outgoing = pair_parts.astype(jnp.bfloat16)
    incoming = [
        lax.ppermute(
            lax.dynamic_index_in_dim(outgoing, (x_index + s) % x_count, 0, keepdims=False),
            "x",
            [(i, (i + s) % x_count) for i in range(x_count)],
        )
        for s in range(1, x_count)
    ]
    panel_reordered = (
        column_panel.reshape(row_count, col_count, slice_rows, tile_cols)
        .transpose(1, 0, 2, 3)
        .reshape(HQ, tile_cols)
    )
    right_gram = lax.dot_general(
        panel_reordered, row_block, (((0,), (0,)), ((), ())), preferred_element_type=jnp.float32
    )
    right_new = stat_decay * right_stat + right_gram * (1.0 / math.sqrt(HQ))
    mixed_rows = lax.all_gather(left_mixed, COL, axis=1, tiled=True)
    incoming, mixed_rows = lax.optimization_barrier((incoming, mixed_rows))
    x_sum = lax.dynamic_index_in_dim(pair_parts, x_index, 0, keepdims=False)
    for part in incoming:
        x_sum = x_sum + part.astype(jnp.float32)
    across = lax.ppermute(
        lax.dynamic_index_in_dim(x_sum, 1 - y_half, 0, keepdims=False).astype(jnp.bfloat16),
        "yh",
        [(0, 1), (1, 0)],
    )
    left_sum = lax.dynamic_index_in_dim(x_sum, y_half, 0, keepdims=False) + across.astype(
        jnp.float32
    )
    update_sum = lax.dot_general(
        mixed_rows, right_root, (((1,), (1,)), ((), ())), preferred_element_type=jnp.float32
    )
    left_new = stat_decay * left_stat + left_sum * (1.0 / math.sqrt(DIN))
    return (left_new, right_new, update_sum.astype(jnp.bfloat16))


def solution(mesh):
    rows, cols = mesh.devices.shape
    split_mesh = Mesh(mesh.devices.reshape(rows // 2, 2, cols // 2, 2), ("x", "yh", "chip", "core"))
    in_specs = (P(ROW, COL, None), P(), P(ROW, COL), P(COL, ROW), P(ROW, None), P(COL, None))
    out_specs = (P(ROW, COL), P(COL, ROW), P(ROW, COL))
    return jax.shard_map(
        shards, mesh=split_mesh, in_specs=in_specs, out_specs=out_specs, check_vma=False
    )
```

profile of v0, /device:TPU:1, one launch (start us, length us, event | category | flops | bytes accessed | tf_op | source)
XLA Modules:
  0.0 226.9 jit_solution(9901679162960642926)
XLA Ops:
  7.2 22.8 %reduce = bf16[524288]{0:T(1024)(128)(2,1)S(1)} reduce(bf16[1,1,524288]{2,1,0:T(2,128)(2,1)} %param.6, bf16[]{:T(256)} %constant.189), dimensions={0,1}, to_apply=%param.6.reduce_sub_computation | reduce | bytes 2097154 | tf_op args[0]
  30.0 0.7 all_to_all.38
  30.6 1.5 copy.25
  32.2 7.8 %all-to-all-start = ((bf16[64,16,512]{2,0,1:T(8,128)(2,1)}), bf16[64,16,512]{2,0,1:T(8,128)(2,1)S(1)}, u32[]{:S(2)}, u32[]{:S(2)}) async-start(bf16[64,16,512]{2,0,1:T(8,128)(2,1)} %copy.25), calls=%async_computation | async-start | bytes 2097152 | tf_op jit(solution)/shard_map/all_to_all | solution.py:44
  40.0 0.7 constant_dynamic-slice_fusion
  40.7 0.2 reduce-window_clone.1
  40.9 0.7 subtract_bitcast_fusion
  41.9 13.9 %all-to-all-done = bf16[64,16,512]{2,0,1:T(8,128)(2,1)S(1)} async-done(((bf16[64,16,512]{2,0,1:T(8,128)(2,1)}), bf16[64,16,512]{2,0,1:T(8,128)(2,1)S(1)}, u32[]{:S(2)}, u32[]{:S(2)}) %all-to-all-start) | async-done | bytes 1048608 | tf_op jit(solution)/shard_map/all_to_all | solution.py:44
  55.9 2.0 gather_fusion
  57.8 0.9 broadcast_select_fusion.1
  58.8 4.2 %all-to-all-start.1 = ((bf16[16,32,512]{2,1,0:T(8,128)(2,1)}), bf16[16,32,512]{2,1,0:T(8,128)(2,1)S(1)}, u32[]{:S(2)}, u32[]{:S(2)}) async-start(bf16[16,32,512]{2,1,0:T(8,128)(2,1)} %broadcast_select_fusion.1), calls=%async_computation.1 | async-start | bytes 1048576 | tf_op jit(solution)/shard_map/all_to_all | solution.py:47
  63.2 2.7 %collective-permute-start = (bf16[512,512]{1,0:T(8,128)(2,1)S(1)}, bf16[512,512]{1,0:T(8,128)(2,1)S(1)}, u32[]{:S(2)}, u32[]{:S(2)}) collective-permute-start(bf16[512,512]{1,0:T(8,128)(2,1)S(1)} %broadcast_select_fusion), channel_id=1, source_target_pairs={{0,16},{16,0},{1,17},{17,1},{2,18},{18,2},{3,19},{19,3},{4,20},{20... | collective-permute-start | bytes 1572872 | tf_op jit(solution)/shard_map/ppermute | solution.py:49
  65.9 7.3 %all-to-all-done.1 = bf16[16,32,512]{2,1,0:T(8,128)(2,1)S(1)} async-done(((bf16[16,32,512]{2,1,0:T(8,128)(2,1)}), bf16[16,32,512]{2,1,0:T(8,128)(2,1)S(1)}, u32[]{:S(2)}, u32[]{:S(2)}) %all-to-all-start.1) | async-done | bytes 524320 | tf_op jit(solution)/shard_map/all_to_all | solution.py:47
  73.2 0.3 copy.26
  73.5 0.2 all_to_all.44
  73.6 1.1 copy.27
  74.7 6.1 %all-to-all-start.2 = ((bf16[32,8,1024]{2,0,1:T(8,128)(2,1)}), bf16[32,8,1024]{2,0,1:T(8,128)(2,1)S(1)}, u32[]{:S(2)}, u32[]{:S(2)}) async-start(bf16[32,8,1024]{2,0,1:T(8,128)(2,1)} %copy.27), calls=%async_computation.2 | async-start | bytes 1048576 | tf_op jit(solution)/shard_map/all_to_all | solution.py:48
  80.8 2.8 %collective-permute-done = bf16[512,512]{1,0:T(8,128)(2,1)S(1)} collective-permute-done((bf16[512,512]{1,0:T(8,128)(2,1)S(1)}, bf16[512,512]{1,0:T(8,128)(2,1)S(1)}, u32[]{:S(2)}, u32[]{:S(2)}) %collective-permute-start) | collective-permute-done | bytes 524320 | tf_op jit(solution)/shard_map/ppermute | solution.py:49
  83.6 5.8 %all-to-all-done.2 = bf16[32,8,1024]{2,0,1:T(8,128)(2,1)S(1)} async-done(((bf16[32,8,1024]{2,0,1:T(8,128)(2,1)}), bf16[32,8,1024]{2,0,1:T(8,128)(2,1)S(1)}, u32[]{:S(2)}, u32[]{:S(2)}) %all-to-all-start.2) | async-done | bytes 524320 | tf_op jit(solution)/shard_map/all_to_all | solution.py:48
  89.4 0.8 copy-done.2
  90.3 0.2 select_bitcast_fusion.1
  90.5 2.3 %broadcast_in_dim.40 = bf16[8,512,512]{2,1,0:T(8,128)(2,1)} broadcast(bf16[]{:T(256)} %constant.160.clone.1), dimensions={} | broadcast | bytes 4194306 | tf_op jit(solution)/shard_map/broadcast_in_dim | solution.py:59
  92.8 1.5 pad_maximum_fusion
  94.3 0.3 collective-permute-start.1
  94.6 1.6 collective-permute-start.2
  96.2 1.3 collective-permute-start.3
  97.5 20.3 %collective-permute-done.1 = bf16[2,512,512]{2,1,0:T(8,128)(2,1)S(1)} collective-permute-done((bf16[2,512,512]{2,1,0:T(8,128)(2,1)}, bf16[2,512,512]{2,1,0:T(8,128)(2,1)S(1)}, u32[]{:S(2)}, u32[]{:S(2)}) %collective-permute-start.1) | collective-permute-done | bytes 1048608 | tf_op jit(solution)/shard_map/ppermute | solution.py:55
  117.8 1.1 constant_dynamic-update-slice_fusion.2
  118.9 19.5 %collective-permute-done.2 = bf16[2,512,512]{2,1,0:T(8,128)(2,1)S(1)} collective-permute-done((bf16[2,512,512]{2,1,0:T(8,128)(2,1)}, bf16[2,512,512]{2,1,0:T(8,128)(2,1)S(1)}, u32[]{:S(2)}, u32[]{:S(2)}) %collective-permute-start.2) | collective-permute-done | bytes 1048608 | tf_op jit(solution)/shard_map/ppermute | solution.py:55
  138.4 1.0 constant_dynamic-update-slice_fusion.1
  139.4 3.5 %collective-permute-done.3 = bf16[2,512,512]{2,1,0:T(8,128)(2,1)S(1)} collective-permute-done((bf16[2,512,512]{2,1,0:T(8,128)(2,1)}, bf16[2,512,512]{2,1,0:T(8,128)(2,1)S(1)}, u32[]{:S(2)}, u32[]{:S(2)}) %collective-permute-start.3) | collective-permute-done | bytes 1048608 | tf_op jit(solution)/shard_map/ppermute | solution.py:55
  142.9 1.1 constant_dynamic-update-slice_fusion
  144.0 5.4 %fusion = bf16[512,512]{0,1:T(8,128)(2,1)} fusion(bf16[4096,512]{1,0:T(8,128)(2,1)} %bitcast.12, bf16[512,4096]{1,0:T(8,128)(2,1)S(1)} %copy-done.4), kind=kOutput, calls=%fused_computation.5 | convolution fusion | flops 2147745792 | bytes 8912896 | tf_op jit(solution)/shard_map/dot_general | solution.py:66
  149.6 4.8 %copy.29 = bf16[16,8,32,512]{3,2,1,0:T(8,128)(2,1)} copy(bf16[16,8,32,512]{3,2,0,1:T(8,128)(2,1)} %bitcast.26) | data formatting | bytes 8388608 | tf_op jit(solution)/shard_map/transpose | solution.py:97
  154.3 6.0 %gather_fusion.1 = bf16[256,1024]{1,0:T(8,128)(2,1)S(1)} fusion(bf16[4096,1024]{1,0:T(8,128)(2,1)} %all-gather.3.cloned.1.call-done, s32[1024]{0:T(1024)S(1)} %pad_clamp_fusion), kind=kCustom, calls=%fused_computation.1 | custom fusion | bytes 1049600 | tf_op jit(solution)/shard_map/jit(_take)/gather | solution.py:79
  160.3 5.9 %fusion.5 = f32[4096,256]{1,0:T(8,128)S(1)} fusion(bf16[4096,1024]{1,0:T(8,128)(2,1)} %all-gather.3.cloned.1.call-done, bf16[256,1024]{1,0:T(8,128)(2,1)S(1)} %gather_fusion.1, pred[256]{0:T(512)(128)(4,1)S(1)} %compare_and_fusion.1), kind=kOutput, calls=%fused_computation.17 | convolution fusion | flops 2147745792 | bytes 13107456 | tf_op jit(solution)/shard_map/dot_general | solution.py:80
  166.3 0.3 copy.28
  166.6 0.2 convert_element_type.36
  167.0 1.8 copy-done
  168.7 1.4 collective-permute-start.4
  170.2 3.0 %collective-permute-start.5 = (bf16[2,512,256]{2,1,0:T(8,128)(2,1)S(1)}, bf16[2,512,256]{2,1,0:T(8,128)(2,1)S(1)}, u32[]{:S(2)}, u32[]{:S(2)}) collective-permute-start(bf16[2,512,256]{2,1,0:T(8,128)(2,1)S(1)} %get-tuple-element.24), channel_id=1, source_target_pairs={{0,64},{32,96},{64,0},{96,32},{1,65},{33,97},{65,1},{97,33},{2,66}... | collective-permute-start | bytes 1572872 | tf_op jit(solution)/shard_map/ppermute | solution.py:88
  173.1 9.5 %multiply_add_fusion = f32[512,1024]{1,0:T(8,128)} fusion(f32[512,1024]{1,0:T(8,128)S(1)} %copy-done.5, bf16[4096,512]{1,0:T(8,128)(2,1)S(1)} %bitcast.60, bf16[4096,1024]{1,0:T(8,128)(2,1)} %all-gather.3.cloned.1.call-done), kind=kOutput, calls=%fused_computation.2 | convolution fusion | flops 4296540160 | bytes 16777216 | tf_op jit(solution)/shard_map/dot_general | solution.py:100
  182.6 13.3 %collective-permute-done.5 = bf16[2,512,256]{2,1,0:T(8,128)(2,1)S(1)} collective-permute-done((bf16[2,512,256]{2,1,0:T(8,128)(2,1)S(1)}, bf16[2,512,256]{2,1,0:T(8,128)(2,1)S(1)}, u32[]{:S(2)}, u32[]{:S(2)}) %collective-permute-start.5) | collective-permute-done | bytes 524320 | tf_op jit(solution)/shard_map/ppermute | solution.py:88
  195.9 7.9 %all-gather.5.cloned.1.call-done = bf16[512,8192]{0,1:T(8,128)(2,1)} async-done(((bf16[512,512]{0,1:T(8,128)(2,1)}), bf16[512,8192]{0,1:T(8,128)(2,1)}) %all-gather.5.cloned.1.call-update) | async-done | bytes 8388624 | tf_op jit(solution)/shard_map/all_gather | solution.py:104
  203.8 1.4 fusion.2
  205.3 2.8 %collective-permute-start.7 = (bf16[512,256]{1,0:T(8,128)(2,1)S(1)}, bf16[512,256]{1,0:T(8,128)(2,1)S(1)}, u32[]{:S(2)}, u32[]{:S(2)}) collective-permute-start(bf16[512,256]{1,0:T(8,128)(2,1)S(1)} %fusion.8), channel_id=1, source_target_pairs={{0,16},{16,0},{1,17},{17,1},{2,18},{18,2},{3,19},{19,3},{4,20},{20... | collective-permute-start | bytes 786440 | tf_op jit(solution)/shard_map/ppermute | solution.py:109
  208.1 11.1 %convolution_convert_fusion = bf16[512,512]{1,0:T(8,128)(2,1)} fusion(bf16[512,8192]{0,1:T(8,128)(2,1)} %all-gather.5.cloned.1.call-done, bf16[512,8192]{1,0:T(8,128)(2,1)} %param.11), kind=kOutput, calls=%fused_computation.3 | convolution fusion | flops 4295229440 | bytes 17301504 | tf_op jit(solution)/shard_map/dot_general | solution.py:117
  219.2 0.9 fusion.4
  (33 shorter events, 0.8 us)
Async XLA Ops:
  32.2 23.7 %all-to-all-start = ((bf16[64,16,512]{2,0,1:T(8,128)(2,1)}), bf16[64,16,512]{2,0,1:T(8,128)(2,1)S(1)}, u32[]{:S(2)}, u32[]{:S(2)}) async-start(bf16[64,16,512]{2,0,1:T(8,128)(2,1)} %copy.25), calls=%async_computation | async-start | bytes 2097152 | tf_op jit(solution)/shard_map/all_to_all | solution.py:44
  58.8 14.4 %all-to-all-start.1 = ((bf16[16,32,512]{2,1,0:T(8,128)(2,1)}), bf16[16,32,512]{2,1,0:T(8,128)(2,1)S(1)}, u32[]{:S(2)}, u32[]{:S(2)}) async-start(bf16[16,32,512]{2,1,0:T(8,128)(2,1)} %broadcast_select_fusion.1), calls=%async_computation.1 | async-start | bytes 1048576 | tf_op jit(solution)/shard_map/all_to_all | solution.py:47
  63.2 20.5 %collective-permute-start = (bf16[512,512]{1,0:T(8,128)(2,1)S(1)}, bf16[512,512]{1,0:T(8,128)(2,1)S(1)}, u32[]{:S(2)}, u32[]{:S(2)}) collective-permute-start(bf16[512,512]{1,0:T(8,128)(2,1)S(1)} %broadcast_select_fusion), channel_id=1, source_target_pairs={{0,16},{16,0},{1,17},{17,1},{2,18},{18,2},{3,19},{19,3},{4,20},{20... | collective-permute-start | bytes 1572872 | tf_op jit(solution)/shard_map/ppermute | solution.py:49
  74.7 14.7 %all-to-all-start.2 = ((bf16[32,8,1024]{2,0,1:T(8,128)(2,1)}), bf16[32,8,1024]{2,0,1:T(8,128)(2,1)S(1)}, u32[]{:S(2)}, u32[]{:S(2)}) async-start(bf16[32,8,1024]{2,0,1:T(8,128)(2,1)} %copy.27), calls=%async_computation.2 | async-start | bytes 1048576 | tf_op jit(solution)/shard_map/all_to_all | solution.py:48
  80.8 68.6 %all-gather.3.cloned.1.call-start = ((), (), s32[]{:S(2)}) async-start(), calls=%async_computation.3 | async-start | bytes 8912896 | tf_op jit(solution)/shard_map/all_gather | solution.py:58
  89.4 0.8 copy-start.2
  90.2 113.6 %all-gather.5.cloned.1.call-start = ((), (), s32[]{:S(2)}) async-start(), calls=%async_computation.4 | async-start | bytes 8912896 | tf_op jit(solution)/shard_map/all_gather | solution.py:104
  94.3 23.6 %collective-permute-start.1 = (bf16[2,512,512]{2,1,0:T(8,128)(2,1)}, bf16[2,512,512]{2,1,0:T(8,128)(2,1)S(1)}, u32[]{:S(2)}, u32[]{:S(2)}) collective-permute-start(bf16[2,512,512]{2,1,0:T(8,128)(2,1)} %get-tuple-element.26), channel_id=1, source_target_pairs={{0,32},{32,64},{64,96},{96,0},{1,33},{33,65},{65,97},{97,1},{2,34}... | collective-permute-start | bytes 3145736 | tf_op jit(solution)/shard_map/ppermute | solution.py:55
  94.6 43.8 %collective-permute-start.2 = (bf16[2,512,512]{2,1,0:T(8,128)(2,1)}, bf16[2,512,512]{2,1,0:T(8,128)(2,1)S(1)}, u32[]{:S(2)}, u32[]{:S(2)}) collective-permute-start(bf16[2,512,512]{2,1,0:T(8,128)(2,1)} %get-tuple-element.26), channel_id=1, source_target_pairs={{0,64},{32,96},{64,0},{96,32},{1,65},{33,97},{65,1},{97,33},{2,66}... | collective-permute-start | bytes 3145736 | tf_op jit(solution)/shard_map/ppermute | solution.py:55
  96.2 46.7 %collective-permute-start.3 = (bf16[2,512,512]{2,1,0:T(8,128)(2,1)}, bf16[2,512,512]{2,1,0:T(8,128)(2,1)S(1)}, u32[]{:S(2)}, u32[]{:S(2)}) collective-permute-start(bf16[2,512,512]{2,1,0:T(8,128)(2,1)} %get-tuple-element.26), channel_id=1, source_target_pairs={{0,96},{32,0},{64,32},{96,64},{1,97},{33,1},{65,33},{97,65},{2,98}... | collective-permute-start | bytes 3145736 | tf_op jit(solution)/shard_map/ppermute | solution.py:55
  97.5 46.5 %copy-start.4 = (bf16[512,4096]{1,0:T(8,128)(2,1)S(1)}, bf16[512,4096]{1,0:T(8,128)(2,1)}, u32[]{:S(2)}) copy-start(bf16[512,4096]{1,0:T(8,128)(2,1)} %param.10) | copy-start | bytes 12582916
  166.6 2.2 copy-start
  166.6 6.5 %copy-start.1 = (bf16[16,8,32,512]{3,2,1,0:T(8,128)(2,1)S(1)}, bf16[16,8,32,512]{3,2,1,0:T(8,128)(2,1)}, u32[]{:S(2)}) copy-start(bf16[16,8,32,512]{3,2,1,0:T(8,128)(2,1)} %copy.29) | copy-start | bytes 12582916
  166.6 6.5 %copy-start.5 = (f32[512,1024]{1,0:T(8,128)S(1)}, f32[512,1024]{1,0:T(8,128)}, u32[]{:S(2)}) copy-start(f32[512,1024]{1,0:T(8,128)} %param.9) | copy-start | bytes 6291460
  168.7 13.9 %collective-permute-start.4 = (bf16[2,512,256]{2,1,0:T(8,128)(2,1)S(1)}, bf16[2,512,256]{2,1,0:T(8,128)(2,1)S(1)}, u32[]{:S(2)}, u32[]{:S(2)}) collective-permute-start(bf16[2,512,256]{2,1,0:T(8,128)(2,1)S(1)} %get-tuple-element.25), channel_id=1, source_target_pairs={{0,32},{32,64},{64,96},{96,0},{1,33},{33,65},{65,97},{97,1},{2,34}... | collective-permute-start | bytes 1572872 | tf_op jit(solution)/shard_map/ppermute | solution.py:88
  170.2 25.7 %collective-permute-start.5 = (bf16[2,512,256]{2,1,0:T(8,128)(2,1)S(1)}, bf16[2,512,256]{2,1,0:T(8,128)(2,1)S(1)}, u32[]{:S(2)}, u32[]{:S(2)}) collective-permute-start(bf16[2,512,256]{2,1,0:T(8,128)(2,1)S(1)} %get-tuple-element.24), channel_id=1, source_target_pairs={{0,64},{32,96},{64,0},{96,32},{1,65},{33,97},{65,1},{97,33},{2,66}... | collective-permute-start | bytes 1572872 | tf_op jit(solution)/shard_map/ppermute | solution.py:88
  173.1 22.8 %collective-permute-start.6 = (bf16[2,512,256]{2,1,0:T(8,128)(2,1)S(1)}, bf16[2,512,256]{2,1,0:T(8,128)(2,1)S(1)}, u32[]{:S(2)}, u32[]{:S(2)}) collective-permute-start(bf16[2,512,256]{2,1,0:T(8,128)(2,1)S(1)} %get-tuple-element.23), channel_id=1, source_target_pairs={{0,96},{32,0},{64,32},{96,64},{1,97},{33,1},{65,33},{97,65},{2,98}... | collective-permute-start | bytes 1572872 | tf_op jit(solution)/shard_map/ppermute | solution.py:88
  205.3 13.9 %copy-start.3 = (f32[512,256]{1,0:T(8,128)S(1)}, f32[512,256]{1,0:T(8,128)}, u32[]{:S(2)}) copy-start(f32[512,256]{1,0:T(8,128)} %param.8) | copy-start | bytes 1572868
  205.3 13.9 %collective-permute-start.7 = (bf16[512,256]{1,0:T(8,128)(2,1)S(1)}, bf16[512,256]{1,0:T(8,128)(2,1)S(1)}, u32[]{:S(2)}, u32[]{:S(2)}) collective-permute-start(bf16[512,256]{1,0:T(8,128)(2,1)S(1)} %fusion.8), channel_id=1, source_target_pairs={{0,16},{16,0},{1,17},{17,1},{2,18},{18,2},{3,19},{19,3},{4,20},{20... | collective-permute-start | bytes 786440 | tf_op jit(solution)/shard_map/ppermute | solution.py:109
Sparse Core Ops, SparseCore 0:
  90.4 52.3 all-gather.2
  149.6 54.1 all-gather.4
where the time goes:
time: 228 us; the launch traced here: 227 us
  waiting for transfers between devices  94.4 us (41%)
  matrix products  31.9 us (14%)
  starting transfers between devices  31.4 us (14%)
  other arithmetic  29.1 us (13%)
  local copies, waits for them, and re-layouts  25.9 us (11%)
  between operations  14.3 us (6%)
    ppermute x3, waiting for transfers between devices, shards(): lax.ppermute(pair, 'x', [(i, (i + s) % x_count) for i in range(x_count)])  43.3 us
    unnamed x1, other arithmetic  22.8 us
    all_to_all x1, waiting for transfers between devices, shards(): lax.all_to_all(held_rows, COL, split_axis=1, concat_axis=0, tiled=True)  13.9 us
    ppermute x3, waiting for transfers between devices, shards(): lax.ppermute(lax.dynamic_index_in_dim(outgoing, (x_index + s) % x_count,...  13.3 us
    dot_general x1, matrix products, shards(): lax.dot_general(mixed_rows, right_root, (((1,), (1,)), ((), ())), preferr...  11.1 us
    dot_general x1, matrix products, shards(): lax.dot_general(panel_reordered, row_block, (((0,), (0,)), ((), ())), pre...  9.46 us
    all_gather x1, waiting for transfers between devices, shards(): mixed_rows = lax.all_gather(left_mixed, COL, axis=1, tiled=True)  7.9 us
    all_to_all x1, starting transfers between devices, shards(): lax.all_to_all(held_rows, COL, split_axis=1, concat_axis=0, tiled=True)  7.84 us
  transfers between devices with their start and end apart: 13, of which 9 were waited for; matrix products, arithmetic and copies ran while one was open for 24% of the time, Pallas kernels for 0%

commit v1 on v0

--- a/solution.py
+++ b/solution.py
@@ -101,7 +101,8 @@
         panel_reordered, row_block, (((0,), (0,)), ((), ())), preferred_element_type=jnp.float32
     )
     right_new = stat_decay * right_stat + right_gram * (1.0 / math.sqrt(HQ))
-    mixed_rows = lax.all_gather(left_mixed, COL, axis=1, tiled=True)
+    sent = jnp.stack([left_mixed] * lax.axis_size(COL))
+    mixed_rows = jnp.concatenate(lax.all_to_all(sent, COL, 0, 0), axis=1)
     incoming, mixed_rows = lax.optimization_barrier((incoming, mixed_rows))
     x_sum = lax.dynamic_index_in_dim(pair_parts, x_index, 0, keepdims=False)
     for part in incoming:

time: 228 us -> 311 us (1.36); the launches traced: 227 us -> 306 us
  waiting for transfers between devices: 94.4 us -> 164 us
  starting transfers between devices: 31.4 us -> 37.2 us
  local copies, waits for them, and re-layouts: 25.9 us -> 29.9 us
    all_to_all x0 -> x1, waiting for transfers between devices: none -> 77 us  [shards(): mixed_rows = jnp.concatenate(lax.all_to_all(sent, COL, 0, 0), axis=1)]
    all_to_all x0 -> x1, starting transfers between devices: none -> 8.52 us  [shards(): mixed_rows = jnp.concatenate(lax.all_to_all(sent, COL, 0, 0), axis=1)]
    all_gather x1 -> x0, waiting for transfers between devices: 7.9 us -> none  [shards(): mixed_rows = lax.all_gather(left_mixed, COL, axis=1, tiled=True)]
    another operation x0 -> x1, local copies, waits for them, and re-layouts: none -> 4.04 us  [shards(): sent = jnp.stack([left_mixed] * lax.axis_size(COL))]
  transfers between devices with their start and end apart: 13 -> 13, of which waited for: 9 -> 11; matrix products, arithmetic and copies ran while one was open for 24% -> 17% of each run, Pallas kernels for 0% -> 0%
where the time goes in v1:
time: 311 us; the launch traced here: 306 us
  waiting for transfers between devices  164 us (53%)
  starting transfers between devices  37.2 us (12%)
  matrix products  30.9 us (10%)
  local copies, waits for them, and re-layouts  29.9 us (10%)
  other arithmetic  29.2 us (9%)
  between operations  14.2 us (5%)
    all_to_all x1, waiting for transfers between devices, shards(): mixed_rows = jnp.concatenate(lax.all_to_all(sent, COL, 0, 0), axis=1)  77 us
    ppermute x3, waiting for transfers between devices, shards(): lax.ppermute(pair, 'x', [(i, (i + s) % x_count) for i in range(x_count)])  43.3 us
    unnamed x1, other arithmetic  22.8 us
    ppermute x3, waiting for transfers between devices, shards(): lax.ppermute(lax.dynamic_index_in_dim(outgoing, (x_index + s) % x_count,...  14.2 us
    all_to_all x1, waiting for transfers between devices, shards(): lax.all_to_all(held_rows, COL, split_axis=1, concat_axis=0, tiled=True)  13.9 us
    dot_general x1, matrix products, shards(): lax.dot_general(mixed_rows, right_root, (((1,), (1,)), ((), ())), preferr...  11.1 us
    dot_general x1, matrix products, shards(): lax.dot_general(panel_reordered, row_block, (((0,), (0,)), ((), ())), pre...  9.3 us
    all_to_all x1, starting transfers between devices, shards(): mixed_rows = jnp.concatenate(lax.all_to_all(sent, COL, 0, 0), axis=1)  8.52 us
  transfers between devices with their start and end apart: 13, of which 11 were waited for; matrix products, arithmetic and copies ran while one was open for 17% of the time, Pallas kernels for 0%

profile of v1, /device:TPU:1, one launch (start us, length us, event | category | flops | bytes accessed | tf_op | source)
XLA Modules:
  0.0 305.7 jit_solution(16287160029643950053)
XLA Ops:
  7.2 22.8 %reduce = bf16[524288]{0:T(1024)(128)(2,1)S(1)} reduce(bf16[1,1,524288]{2,1,0:T(2,128)(2,1)} %param.6, bf16[]{:T(256)} %constant.189), dimensions={0,1}, to_apply=%param.6.reduce_sub_computation | reduce | bytes 2097154 | tf_op args[0]
  30.0 0.7 all_to_all.41
  30.6 1.5 copy.26
  32.2 7.8 %all-to-all-start = ((bf16[64,16,512]{2,0,1:T(8,128)(2,1)}), bf16[64,16,512]{2,0,1:T(8,128)(2,1)S(1)}, u32[]{:S(2)}, u32[]{:S(2)}) async-start(bf16[64,16,512]{2,0,1:T(8,128)(2,1)} %copy.26), calls=%async_computation | async-start | bytes 2097152 | tf_op jit(solution)/shard_map/all_to_all | solution.py:44
  40.0 0.7 constant_dynamic-slice_fusion
  40.9 0.7 subtract_bitcast_fusion
  41.9 13.9 %all-to-all-done = bf16[64,16,512]{2,0,1:T(8,128)(2,1)S(1)} async-done(((bf16[64,16,512]{2,0,1:T(8,128)(2,1)}), bf16[64,16,512]{2,0,1:T(8,128)(2,1)S(1)}, u32[]{:S(2)}, u32[]{:S(2)}) %all-to-all-start) | async-done | bytes 1048608 | tf_op jit(solution)/shard_map/all_to_all | solution.py:44
  55.9 2.0 gather_fusion
  57.8 0.9 broadcast_select_fusion.1
  58.8 4.2 %all-to-all-start.1 = ((bf16[16,32,512]{2,1,0:T(8,128)(2,1)}), bf16[16,32,512]{2,1,0:T(8,128)(2,1)S(1)}, u32[]{:S(2)}, u32[]{:S(2)}) async-start(bf16[16,32,512]{2,1,0:T(8,128)(2,1)} %broadcast_select_fusion.1), calls=%async_computation.1 | async-start | bytes 1048576 | tf_op jit(solution)/shard_map/all_to_all | solution.py:47
  63.2 2.7 collective-permute-start
  65.9 7.3 %all-to-all-done.1 = bf16[16,32,512]{2,1,0:T(8,128)(2,1)S(1)} async-done(((bf16[16,32,512]{2,1,0:T(8,128)(2,1)}), bf16[16,32,512]{2,1,0:T(8,128)(2,1)S(1)}, u32[]{:S(2)}, u32[]{:S(2)}) %all-to-all-start.1) | async-done | bytes 524320 | tf_op jit(solution)/shard_map/all_to_all | solution.py:47
  73.2 0.3 copy.27
  73.6 1.1 copy.28
  74.7 6.1 %all-to-all-start.2 = ((bf16[32,8,1024]{2,0,1:T(8,128)(2,1)}), bf16[32,8,1024]{2,0,1:T(8,128)(2,1)S(1)}, u32[]{:S(2)}, u32[]{:S(2)}) async-start(bf16[32,8,1024]{2,0,1:T(8,128)(2,1)} %copy.28), calls=%async_computation.2 | async-start | bytes 1048576 | tf_op jit(solution)/shard_map/all_to_all | solution.py:48
  80.8 2.8 collective-permute-done
  83.6 5.8 %all-to-all-done.2 = bf16[32,8,1024]{2,0,1:T(8,128)(2,1)S(1)} async-done(((bf16[32,8,1024]{2,0,1:T(8,128)(2,1)}), bf16[32,8,1024]{2,0,1:T(8,128)(2,1)S(1)}, u32[]{:S(2)}, u32[]{:S(2)}) %all-to-all-start.2) | async-done | bytes 524320 | tf_op jit(solution)/shard_map/all_to_all | solution.py:48
  89.4 0.8 copy-done.2
  90.4 2.3 broadcast_in_dim.40
  92.8 1.6 pad_maximum_fusion
  94.5 1.7 collective-permute-start.2
  96.2 1.3 collective-permute-start.3
  97.5 20.4 %collective-permute-done.1 = bf16[2,512,512]{2,1,0:T(8,128)(2,1)S(1)} collective-permute-done((bf16[2,512,512]{2,1,0:T(8,128)(2,1)}, bf16[2,512,512]{2,1,0:T(8,128)(2,1)S(1)}, u32[]{:S(2)}, u32[]{:S(2)}) %collective-permute-start.1) | collective-permute-done | bytes 1048608 | tf_op jit(solution)/shard_map/ppermute | solution.py:55
  117.9 1.1 constant_dynamic-update-slice_fusion.2
  119.0 19.4 %collective-permute-done.2 = bf16[2,512,512]{2,1,0:T(8,128)(2,1)S(1)} collective-permute-done((bf16[2,512,512]{2,1,0:T(8,128)(2,1)}, bf16[2,512,512]{2,1,0:T(8,128)(2,1)S(1)}, u32[]{:S(2)}, u32[]{:S(2)}) %collective-permute-start.2) | collective-permute-done | bytes 1048608 | tf_op jit(solution)/shard_map/ppermute | solution.py:55
  138.4 1.0 constant_dynamic-update-slice_fusion.1
  139.4 3.5 %collective-permute-done.3 = bf16[2,512,512]{2,1,0:T(8,128)(2,1)S(1)} collective-permute-done((bf16[2,512,512]{2,1,0:T(8,128)(2,1)}, bf16[2,512,512]{2,1,0:T(8,128)(2,1)S(1)}, u32[]{:S(2)}, u32[]{:S(2)}) %collective-permute-start.3) | collective-permute-done | bytes 1048608 | tf_op jit(solution)/shard_map/ppermute | solution.py:55
  143.0 1.0 constant_dynamic-update-slice_fusion
  144.0 4.6 %fusion = bf16[512,512]{0,1:T(8,128)(2,1)S(1)} fusion(bf16[4096,512]{1,0:T(8,128)(2,1)} %bitcast.12, bf16[512,4096]{1,0:T(8,128)(2,1)S(1)} %copy-done.4), kind=kOutput, calls=%fused_computation.5 | convolution fusion | flops 2147745792 | bytes 8912896 | tf_op jit(solution)/shard_map/dot_general | solution.py:66
  148.7 4.0 %stack.11 = bf16[16,512,512]{1,2,0:T(8,128)(2,1)} broadcast(bf16[512,512]{0,1:T(8,128)(2,1)S(1)} %fusion), dimensions={1,2} | broadcast | bytes 8912896 | tf_op jit(solution)/shard_map/stack | solution.py:104
  152.7 8.5 %all-to-all-start.3 = ((bf16[16,512,512]{1,2,0:T(8,128)(2,1)}), bf16[16,512,512]{1,2,0:T(8,128)(2,1)}, u32[]{:S(2)}, u32[]{:S(2)}) async-start(bf16[16,512,512]{1,2,0:T(8,128)(2,1)} %stack.11), calls=%async_computation.3 | async-start | bytes 16777216 | tf_op jit(solution)/shard_map/all_to_all | solution.py:105
  161.3 4.7 %copy.30 = bf16[16,8,32,512]{3,2,1,0:T(8,128)(2,1)} copy(bf16[16,8,32,512]{3,2,0,1:T(8,128)(2,1)} %bitcast.28) | data formatting | bytes 8388608 | tf_op jit(solution)/shard_map/transpose | solution.py:97
  166.0 6.0 %gather_fusion.1 = bf16[256,1024]{1,0:T(8,128)(2,1)S(1)} fusion(bf16[4096,1024]{1,0:T(8,128)(2,1)} %all-gather.2.cloned.1.call-done, s32[1024]{0:T(1024)S(1)} %pad_clamp_fusion), kind=kCustom, calls=%fused_computation.1 | custom fusion | bytes 1049600 | tf_op jit(solution)/shard_map/jit(_take)/gather | solution.py:79
  172.0 5.8 %fusion.5 = f32[4096,256]{1,0:T(8,128)S(1)} fusion(bf16[4096,1024]{1,0:T(8,128)(2,1)} %all-gather.2.cloned.1.call-done, bf16[256,1024]{1,0:T(8,128)(2,1)S(1)} %gather_fusion.1, pred[256]{0:T(512)(128)(4,1)S(1)} %compare_and_fusion.1), kind=kOutput, calls=%fused_computation.17 | convolution fusion | flops 2147745792 | bytes 13107456 | tf_op jit(solution)/shard_map/dot_general | solution.py:80
  177.9 0.3 copy.29
  178.2 0.2 convert_element_type.36
  178.6 1.8 copy-done
  180.3 2.1 collective-permute-start.5
  182.4 0.6 collective-permute-start.6
  183.0 9.3 %multiply_add_fusion = f32[512,1024]{1,0:T(8,128)} fusion(f32[512,1024]{1,0:T(8,128)S(1)} %copy-done.5, bf16[4096,512]{1,0:T(8,128)(2,1)S(1)} %bitcast.63, bf16[4096,1024]{1,0:T(8,128)(2,1)} %all-gather.2.cloned.1.call-done), kind=kOutput, calls=%fused_computation.2 | convolution fusion | flops 4296540160 | bytes 16777216 | tf_op jit(solution)/shard_map/dot_general | solution.py:100
  192.3 3.2 %collective-permute-done.4 = bf16[2,512,256]{2,1,0:T(8,128)(2,1)S(1)} collective-permute-done((bf16[2,512,256]{2,1,0:T(8,128)(2,1)S(1)}, bf16[2,512,256]{2,1,0:T(8,128)(2,1)S(1)}, u32[]{:S(2)}, u32[]{:S(2)}) %collective-permute-start.4) | collective-permute-done | bytes 524320 | tf_op jit(solution)/shard_map/ppermute | solution.py:88
  195.5 10.1 %collective-permute-done.5 = bf16[2,512,256]{2,1,0:T(8,128)(2,1)S(1)} collective-permute-done((bf16[2,512,256]{2,1,0:T(8,128)(2,1)S(1)}, bf16[2,512,256]{2,1,0:T(8,128)(2,1)S(1)}, u32[]{:S(2)}, u32[]{:S(2)}) %collective-permute-start.5) | collective-permute-done | bytes 524320 | tf_op jit(solution)/shard_map/ppermute | solution.py:88
  205.6 0.8 collective-permute-done.6
  206.5 77.0 %all-to-all-done.3 = bf16[16,512,512]{1,2,0:T(8,128)(2,1)} async-done(((bf16[16,512,512]{1,2,0:T(8,128)(2,1)}), bf16[16,512,512]{1,2,0:T(8,128)(2,1)}, u32[]{:S(2)}, u32[]{:S(2)}) %all-to-all-start.3) | async-done | bytes 8388640 | tf_op jit(solution)/shard_map/all_to_all | solution.py:105
  283.5 1.4 fusion.2
  285.0 1.9 collective-permute-start.7
  286.9 11.1 %convolution_convert_fusion = bf16[512,512]{1,0:T(8,128)(2,1)} fusion(bf16[512,8192]{0,1:T(8,128)(2,1)} %bitcast.24, bf16[512,8192]{1,0:T(8,128)(2,1)} %param.11), kind=kOutput, calls=%fused_computation.3 | convolution fusion | flops 4295229440 | bytes 17301504 | tf_op jit(solution)/shard_map/dot_general | solution.py:118
  298.0 0.9 fusion.4
  (33 shorter events, 1.5 us)
Async XLA Ops:
  32.2 23.7 %all-to-all-start = ((bf16[64,16,512]{2,0,1:T(8,128)(2,1)}), bf16[64,16,512]{2,0,1:T(8,128)(2,1)S(1)}, u32[]{:S(2)}, u32[]{:S(2)}) async-start(bf16[64,16,512]{2,0,1:T(8,128)(2,1)} %copy.26), calls=%async_computation | async-start | bytes 2097152 | tf_op jit(solution)/shard_map/all_to_all | solution.py:44
  58.8 14.4 %all-to-all-start.1 = ((bf16[16,32,512]{2,1,0:T(8,128)(2,1)}), bf16[16,32,512]{2,1,0:T(8,128)(2,1)S(1)}, u32[]{:S(2)}, u32[]{:S(2)}) async-start(bf16[16,32,512]{2,1,0:T(8,128)(2,1)} %broadcast_select_fusion.1), calls=%async_computation.1 | async-start | bytes 1048576 | tf_op jit(solution)/shard_map/all_to_all | solution.py:47
  63.2 20.5 %collective-permute-start = (bf16[512,512]{1,0:T(8,128)(2,1)S(1)}, bf16[512,512]{1,0:T(8,128)(2,1)S(1)}, u32[]{:S(2)}, u32[]{:S(2)}) collective-permute-start(bf16[512,512]{1,0:T(8,128)(2,1)S(1)} %broadcast_select_fusion), channel_id=1, source_target_pairs={{0,16},{16,0},{1,17},{17,1},{2,18},{18,2},{3,19},{19,3},{4,20},{20... | collective-permute-start | bytes 1572872 | tf_op jit(solution)/shard_map/ppermute | solution.py:49
  74.7 14.7 %all-to-all-start.2 = ((bf16[32,8,1024]{2,0,1:T(8,128)(2,1)}), bf16[32,8,1024]{2,0,1:T(8,128)(2,1)S(1)}, u32[]{:S(2)}, u32[]{:S(2)}) async-start(bf16[32,8,1024]{2,0,1:T(8,128)(2,1)} %copy.28), calls=%async_computation.2 | async-start | bytes 1048576 | tf_op jit(solution)/shard_map/all_to_all | solution.py:48
  80.8 67.9 %all-gather.2.cloned.1.call-start = ((), (), s32[]{:S(2)}) async-start(), calls=%async_computation.4 | async-start | bytes 8912896 | tf_op jit(solution)/shard_map/all_gather | solution.py:58
  89.4 0.8 copy-start.2
  94.3 23.6 %collective-permute-start.1 = (bf16[2,512,512]{2,1,0:T(8,128)(2,1)}, bf16[2,512,512]{2,1,0:T(8,128)(2,1)S(1)}, u32[]{:S(2)}, u32[]{:S(2)}) collective-permute-start(bf16[2,512,512]{2,1,0:T(8,128)(2,1)} %get-tuple-element.26), channel_id=1, source_target_pairs={{0,32},{32,64},{64,96},{96,0},{1,33},{33,65},{65,97},{97,1},{2,34}... | collective-permute-start | bytes 3145736 | tf_op jit(solution)/shard_map/ppermute | solution.py:55
  94.5 43.9 %collective-permute-start.2 = (bf16[2,512,512]{2,1,0:T(8,128)(2,1)}, bf16[2,512,512]{2,1,0:T(8,128)(2,1)S(1)}, u32[]{:S(2)}, u32[]{:S(2)}) collective-permute-start(bf16[2,512,512]{2,1,0:T(8,128)(2,1)} %get-tuple-element.26), channel_id=1, source_target_pairs={{0,64},{32,96},{64,0},{96,32},{1,65},{33,97},{65,1},{97,33},{2,66}... | collective-permute-start | bytes 3145736 | tf_op jit(solution)/shard_map/ppermute | solution.py:55
  96.2 46.8 %collective-permute-start.3 = (bf16[2,512,512]{2,1,0:T(8,128)(2,1)}, bf16[2,512,512]{2,1,0:T(8,128)(2,1)S(1)}, u32[]{:S(2)}, u32[]{:S(2)}) collective-permute-start(bf16[2,512,512]{2,1,0:T(8,128)(2,1)} %get-tuple-element.26), channel_id=1, source_target_pairs={{0,96},{32,0},{64,32},{96,64},{1,97},{33,1},{65,33},{97,65},{2,98}... | collective-permute-start | bytes 3145736 | tf_op jit(solution)/shard_map/ppermute | solution.py:55
  97.5 46.5 %copy-start.4 = (bf16[512,4096]{1,0:T(8,128)(2,1)S(1)}, bf16[512,4096]{1,0:T(8,128)(2,1)}, u32[]{:S(2)}) copy-start(bf16[512,4096]{1,0:T(8,128)(2,1)} %param.10) | copy-start | bytes 12582916
  152.7 130.8 %all-to-all-start.3 = ((bf16[16,512,512]{1,2,0:T(8,128)(2,1)}), bf16[16,512,512]{1,2,0:T(8,128)(2,1)}, u32[]{:S(2)}, u32[]{:S(2)}) async-start(bf16[16,512,512]{1,2,0:T(8,128)(2,1)} %stack.11), calls=%async_computation.3 | async-start | bytes 16777216 | tf_op jit(solution)/shard_map/all_to_all | solution.py:105
  178.2 2.1 copy-start
  178.2 4.8 %copy-start.1 = (bf16[16,8,32,512]{3,2,1,0:T(8,128)(2,1)S(1)}, bf16[16,8,32,512]{3,2,1,0:T(8,128)(2,1)}, u32[]{:S(2)}) copy-start(bf16[16,8,32,512]{3,2,1,0:T(8,128)(2,1)} %copy.30) | copy-start | bytes 12582916
  178.2 4.8 %copy-start.5 = (f32[512,1024]{1,0:T(8,128)S(1)}, f32[512,1024]{1,0:T(8,128)}, u32[]{:S(2)}) copy-start(f32[512,1024]{1,0:T(8,128)} %param.9) | copy-start | bytes 6291460
  180.3 15.2 %collective-permute-start.4 = (bf16[2,512,256]{2,1,0:T(8,128)(2,1)S(1)}, bf16[2,512,256]{2,1,0:T(8,128)(2,1)S(1)}, u32[]{:S(2)}, u32[]{:S(2)}) collective-permute-start(bf16[2,512,256]{2,1,0:T(8,128)(2,1)S(1)} %get-tuple-element.25), channel_id=1, source_target_pairs={{0,32},{32,64},{64,96},{96,0},{1,33},{33,65},{65,97},{97,1},{2,34}... | collective-permute-start | bytes 1572872 | tf_op jit(solution)/shard_map/ppermute | solution.py:88
  180.3 25.3 %collective-permute-start.5 = (bf16[2,512,256]{2,1,0:T(8,128)(2,1)S(1)}, bf16[2,512,256]{2,1,0:T(8,128)(2,1)S(1)}, u32[]{:S(2)}, u32[]{:S(2)}) collective-permute-start(bf16[2,512,256]{2,1,0:T(8,128)(2,1)S(1)} %get-tuple-element.24), channel_id=1, source_target_pairs={{0,64},{32,96},{64,0},{96,32},{1,65},{33,97},{65,1},{97,33},{2,66}... | collective-permute-start | bytes 1572872 | tf_op jit(solution)/shard_map/ppermute | solution.py:88
  182.4 24.1 %collective-permute-start.6 = (bf16[2,512,256]{2,1,0:T(8,128)(2,1)S(1)}, bf16[2,512,256]{2,1,0:T(8,128)(2,1)S(1)}, u32[]{:S(2)}, u32[]{:S(2)}) collective-permute-start(bf16[2,512,256]{2,1,0:T(8,128)(2,1)S(1)} %get-tuple-element.23), channel_id=1, source_target_pairs={{0,96},{32,0},{64,32},{96,64},{1,97},{33,1},{65,33},{97,65},{2,98}... | collective-permute-start | bytes 1572872 | tf_op jit(solution)/shard_map/ppermute | solution.py:88
  285.0 13.0 %copy-start.3 = (f32[512,256]{1,0:T(8,128)S(1)}, f32[512,256]{1,0:T(8,128)}, u32[]{:S(2)}) copy-start(f32[512,256]{1,0:T(8,128)} %param.8) | copy-start | bytes 1572868
  285.0 13.0 %collective-permute-start.7 = (bf16[512,256]{1,0:T(8,128)(2,1)S(1)}, bf16[512,256]{1,0:T(8,128)(2,1)S(1)}, u32[]{:S(2)}, u32[]{:S(2)}) collective-permute-start(bf16[512,256]{1,0:T(8,128)(2,1)S(1)} %fusion.8), channel_id=1, source_target_pairs={{0,16},{16,0},{1,17},{17,1},{2,18},{18,2},{3,19},{19,3},{4,20},{20... | collective-permute-start | bytes 786440 | tf_op jit(solution)/shard_map/ppermute | solution.py:110
Sparse Core Ops, SparseCore 0:
  90.4 52.3 all-gather.1
